TPU v7x, 256 devices: a whole 4x4x8 slice. The times are simulated.
256 devices in a mesh: member: 8 (over x, y_hi), space: 32 (over y_lo, z, core).
Axes of the slice: x: 4, y: 4 (y_hi: 2, y_lo: 2; y = y_hi * 2 + y_lo), z: 8, core: 2. Of those that a mesh axis runs over, the one named last changes fastest.
Arguments:
- ensemble: bfloat16 [256, 48, 16384], P('member', None, 'space')
- inflation: float32 [256, 128], P('member'), may hold values from 0.5 to 2
- weights: bfloat16 [128, 256, 256], P('space')
- region_ids: int32 [16384], P('space'), may hold values from 0 to 127, as said below
- extinction: float32 [48], replicated, may hold values from 0.1 to 2
- obs_cols: int32 [4096], P('space'), may hold values from 0 to 16383, as said below
Outputs:
- analysis: bfloat16 [256, 48, 16384], P('member', None, 'space')
- obs_analysis: float32 [256, 4096], P('member', 'space')
Inputs may be any that keep to these rules, and one draw needn't show every extreme that they name: `region_ids`: region r belongs to index r // 4 of space. Each block of 512 columns held by one index of space holds exactly 16 columns of the regions of every index of space. `obs_cols`: each observation's column lies in the block of 512 columns held by the same index of space as the observation.
All inputs are finite; a program needn't handle non-finite values.
Results may differ from a plain program's by a relative error of at most 0.0047.
Values may be sent and summed in bfloat16 or wider, within the bound.
No kernel may reach another device: no remote copies, remote signals or barrier semaphores. Data moves between devices by JAX's collectives and lax.ppermute only.
A program may use at most 64 MiB of HBM per device.

v0:
```python
import jax
import jax.numpy as jnp
from jax import lax
from jax.sharding import PartitionSpec as P


def local(ensemble, inflation, weights, region_ids, extinction, obs_cols):
    n_space = lax.axis_size("space")
    n_member = lax.axis_size("member")
    local_members = ensemble.shape[0]
    tracers = ensemble.shape[1]
    columns = ensemble.shape[2]
    members = local_members * n_member
    reg_count = weights.shape[0]
    all_regions = inflation.shape[1]
    send_cols = columns // n_space
    slot_cols = send_cols // n_member
    own_cols = n_space * slot_cols
    owner = region_ids // reg_count
    owner_hot = (owner[:, None] == jnp.arange(n_space, dtype=jnp.int32)[None, :]).astype(jnp.int32)
    before = jnp.cumsum(owner_hot, axis=0) - owner_hot
    rank_in = jnp.sum(before * owner_hot, axis=1)
    position = owner * send_cols + rank_in
    ordering = (
        jnp.zeros((columns,), jnp.int32).at[position].set(jnp.arange(columns, dtype=jnp.int32))
    )
    labels_all = jnp.take(region_ids % reg_count, ordering).reshape(n_space, n_member, slot_cols)
    my_labels = lax.dynamic_index_in_dim(labels_all, lax.axis_index("member"), 1, keepdims=False)
    got_labels = lax.all_to_all(
        my_labels, "space", split_axis=0, concat_axis=0, tiled=True
    ).reshape(own_cols)
    summed = lax.psum(jnp.sum(ensemble, axis=0, dtype=jnp.float32), "member")
    mean = summed / members
    region_hot = (jnp.arange(all_regions, dtype=jnp.int32)[:, None] == region_ids[None, :]).astype(
        jnp.float32
    )
    factor = jnp.dot(inflation, region_hot, precision=lax.Precision.HIGHEST)
    outgoing = ((ensemble.astype(jnp.float32) - mean[None]) * factor[:, None, :]).astype(
        jnp.bfloat16
    )
    rows_major = jnp.transpose(outgoing, (2, 0, 1)).reshape(columns, local_members * tracers)
    payload = jnp.take(rows_major, ordering, axis=0).reshape(
        n_space, n_member, slot_cols, local_members * tracers
    )
    received = lax.all_to_all(
        lax.all_to_all(payload, "member", split_axis=1, concat_axis=3, tiled=True),
        "space",
        split_axis=0,
        concat_axis=0,
        tiled=True,
    )
    gathered = received.reshape(own_cols, members, tracers)
    accum = jnp.zeros((own_cols, members, tracers), jnp.float32)
    for region in range(reg_count):
        partial_prod = jnp.einsum(
            "jk,cjt->ckt", weights[region], gathered, preferred_element_type=jnp.float32
        )
        accum = accum + jnp.where((got_labels == region)[:, None, None], partial_prod, 0.0)
    increment = accum.astype(jnp.bfloat16)
    result_rows = increment
    result_rows = result_rows.reshape(n_space, 1, slot_cols, members * tracers)
    halfway = lax.all_to_all(result_rows, "space", split_axis=0, concat_axis=0, tiled=True)
    returned = lax.all_to_all(halfway, "member", split_axis=3, concat_axis=1, tiled=True)
    restored = jnp.take(returned.reshape(columns, local_members * tracers), position, axis=0)
    restored = jnp.transpose(restored.reshape(columns, local_members, tracers), (1, 2, 0))
    analysis = (mean[None] + restored.astype(jnp.float32)).astype(jnp.bfloat16)
    local_index = obs_cols - lax.axis_index("space") * columns
    picked = jnp.take(analysis, local_index, axis=2).astype(jnp.float32)
    obs_analysis = jnp.einsum("t,kto->ko", extinction, picked, precision=lax.Precision.HIGHEST)
    return (analysis, obs_analysis)


def solution(mesh):
    in_specs = (
        P("member", None, "space"),
        P("member", None),
        P("space", None, None),
        P("space"),
        P(),
        P("space"),
    )
    out_specs = (P("member", None, "space"), P("member", "space"))
    return jax.shard_map(local, mesh=mesh, in_specs=in_specs, out_specs=out_specs, check_vma=False)
```

profile of v0, /device:TPU:64, one launch (start us, length us, event | category | flops | bytes accessed | tf_op | source)
XLA Modules:
  0.0 389.3 jit_solution(15727001249137828852)
XLA Ops:
  7.2 0.0 copy-start
  7.2 0.0 all-reduce.2.cloned.1.call-start
  7.2 7.2 %copy.60 = bf16[32,48,512]{1,0,2:T(8,128)(2,1)} copy(bf16[32,48,512]{2,1,0:T(8,128)(2,1)} %param.8) | data formatting | bytes 3145728 | tf_op args[0]
  14.5 4.8 %convert_reduce_fusion = f32[48,512]{0,1:T(8,128)} fusion(bf16[32,48,512]{1,0,2:T(8,128)(2,1)} %copy.60), kind=kLoop, calls=%fused_computation.6 | loop fusion | flops 1548288 | bytes 1671168 | tf_op jit(solution)/shard_map/reduce_sum | solution.py:32
  19.2 0.0 all-reduce.2.cloned.1.call-update
  19.3 0.0 copy-done.4
  19.3 1.2 reduce-window.6
  20.5 0.2 slice_reduce_fusion
  20.7 0.1 fusion.21
  20.9 2.4 scatter_custom_fusion
  23.3 0.0 copy-done
  23.3 0.2 convolution_bitcast_fusion
  23.6 3.5 gather_fusion
  27.1 0.1 copy.62
  27.2 83.8 %all-reduce.2.cloned.1.call-done = f32[48,512]{0,1:T(8,128)} async-done(((f32[48,512]{0,1:T(8,128)}), f32[48,512]{0,1:T(8,128)}) %all-reduce.2.cloned.1.call-update) | async-done | bytes 98320 | tf_op jit(solution)/shard_map/psum | solution.py:32
  111.0 1.0 broadcast_multiply_fusion
  112.0 5.8 %fusion.3 = bf16[512,32,48]{2,1,0:T(8,128)(2,1)} fusion(bf16[32,48,512]{1,0,2:T(8,128)(2,1)} %copy.60, f32[32,512]{0,1:T(8,128)S(1)} %copy.62, f32[48,512]{0,1:T(8,128)S(1)} %broadcast_multiply_fusion), kind=kLoop, calls=%fused_computation.11 | loop fusion | flops 3145728 | bytes 3309568 | tf_op jit(solution)/shard_map/transpose | solution.py:41
  117.8 4.4 %copy.63 = bf16[512,32,48]{0,2,1:T(8,128)(2,1)S(1)} copy(bf16[512,32,48]{2,1,0:T(8,128)(2,1)} %fusion.3) | data formatting | bytes 3145728 | tf_op jit(solution)/shard_map/transpose | solution.py:41
  122.3 0.7 copy.64
  123.0 2.9 gather_fusion.2
  125.9 1.6 broadcast_select_fusion
  127.6 0.6 reshape.100
  128.2 2.4 copy.65
  130.6 3.6 all-to-all-start.1
  134.1 0.1 select_n.68
  134.3 0.6 constant_dynamic-slice_fusion
  134.9 16.7 %all-to-all-done.1 = bf16[32,8,2,1536]{3,2,0,1:T(2,128)(2,1)S(1)} async-done(((bf16[32,8,2,1536]{3,2,0,1:T(2,128)(2,1)}), bf16[32,8,2,1536]{3,2,0,1:T(2,128)(2,1)S(1)}, u32[]{:S(2)}, u32[]{:S(2)}) %all-to-all-start.1) | async-done | bytes 1572896 | tf_op jit(solution)/shard_map/all_to_all | solution.py:46
  151.6 8.0 %all-to-all-start = ((s32[32,1,2]{2,1,0:T(1,128)}), s32[32,1,2]{2,1,0:T(1,128)S(1)}, u32[]{:S(2)}, u32[]{:S(2)}) async-start(s32[32,1,2]{2,1,0:T(1,128)} %constant_dynamic-slice_fusion), calls=%async_computation | async-start | bytes 32768 | tf_op jit(solution)/shard_map/all_to_all | solution.py:29
  159.6 1.3 copy.85
  160.9 2.1 reshape.160
  163.0 2.8 all-to-all-done
  165.8 6.0 %all-to-all-start.2 = ((bf16[32,1,2,12288]{3,2,1,0:T(2,128)(2,1)}), bf16[32,1,2,12288]{3,2,1,0:T(2,128)(2,1)S(1)}, u32[]{:S(2)}, u32[]{:S(2)}) async-start(bf16[32,1,2,12288]{3,2,1,0:T(2,128)(2,1)} %reshape.160), calls=%async_computation.2 | async-start | bytes 3145728 | tf_op jit(solution)/shard_map/all_to_all | solution.py:45
  171.8 0.0 copy-start.3
  171.8 0.2 compare_reduce_fusion.3
  172.0 0.1 eq.105
  172.1 0.1 eq.108
  172.3 0.1 eq.111
  172.4 0.1 eq.99
  172.5 37.2 %all-to-all-done.2 = bf16[32,1,2,12288]{3,2,1,0:T(2,128)(2,1)S(1)} async-done(((bf16[32,1,2,12288]{3,2,1,0:T(2,128)(2,1)}), bf16[32,1,2,12288]{3,2,1,0:T(2,128)(2,1)S(1)}, u32[]{:S(2)}, u32[]{:S(2)}) %all-to-all-start.2) | async-done | bytes 1572896 | tf_op jit(solution)/shard_map/all_to_all | solution.py:45
  209.6 5.2 %reshape.101 = bf16[64,256,48]{2,1,0:T(8,128)(2,1)} reshape(bf16[32,1,2,12288]{3,2,1,0:T(2,128)(2,1)S(1)} %all-to-all-done.2) | data formatting | bytes 3145728 | tf_op jit(solution)/shard_map/reshape | solution.py:52
  214.8 3.6 fusion.10
  218.4 1.3 fusion.12
  219.7 1.3 fusion.8
  221.0 2.3 fusion.4
  223.3 3.2 copy.72
  226.4 9.3 %reshape.102 = bf16[32,1,2,12288]{3,2,0,1:T(2,128)(2,1)S(1)} reshape(bf16[64,256,48]{2,1,0:T(8,128)(2,1)} %copy.72) | data formatting | bytes 3145728 | tf_op jit(solution)/shard_map/reshape | solution.py:61
  235.7 44.2 %all_to_all.49 = bf16[32,1,2,12288]{3,2,1,0:T(2,128)(2,1)S(1)} all-to-all(bf16[32,1,2,12288]{3,2,1,0:T(2,128)(2,1)S(1)} %bitcast.79), channel_id=1, replica_groups=mesh['member'=8,'space'=32] {'space'}, dimensions={0} | all-to-all | bytes 3145728 | tf_op jit(solution)/shard_map/all_to_all | solution.py:62
  280.0 11.1 %copy.74 = bf16[32,1,2,12288]{0,2,1,3:T(2,128)(2,1)} copy(bf16[32,1,2,12288]{3,2,1,0:T(2,128)(2,1)S(1)} %all_to_all.49) | data formatting | bytes 3145728 | tf_op jit(solution)/shard_map/all_to_all | solution.py:62
  291.1 9.5 %reshape.168 = bf16[8,2,49152]{2,1,0:T(2,128)(2,1)} reshape(bf16[12288,1,2,32]{3,2,1,0:T(2,128)(2,1)} %bitcast.74) | data formatting | bytes 3145728
  300.6 4.8 %all-to-all-start.4 = ((bf16[8,2,49152]{2,1,0:T(2,128)(2,1)}), bf16[8,2,49152]{2,1,0:T(2,128)(2,1)S(1)}, u32[]{:S(2)}, u32[]{:S(2)}) async-start(bf16[8,2,49152]{2,1,0:T(2,128)(2,1)} %reshape.168), calls=%async_computation.4 | async-start | bytes 3145728 | tf_op jit(solution)/shard_map/all_to_all | solution.py:63
  305.4 0.0 copy-done.6
  305.4 24.0 %all-to-all-done.4 = bf16[8,2,49152]{2,1,0:T(2,128)(2,1)S(1)} async-done(((bf16[8,2,49152]{2,1,0:T(2,128)(2,1)}), bf16[8,2,49152]{2,1,0:T(2,128)(2,1)S(1)}, u32[]{:S(2)}, u32[]{:S(2)}) %all-to-all-start.4) | async-done | bytes 1572896 | tf_op jit(solution)/shard_map/all_to_all | solution.py:63
  329.4 5.4 %reshape.169 = bf16[12288,1,2,32]{3,2,1,0:T(2,128)(2,1)} reshape(bf16[8,2,49152]{2,1,0:T(2,128)(2,1)S(1)} %all-to-all-done.4) | data formatting | bytes 3145728
  334.9 14.4 %copy.75 = bf16[32,1,2,8,1536]{4,2,3,0,1:T(2,128)(2,1)S(1)} copy(bf16[32,1,2,8,1536]{0,2,4,3,1:T(2,128)(2,1)} %bitcast.75) | data formatting | bytes 3145728 | tf_op jit(solution)/shard_map/all_to_all | solution.py:63
  349.3 0.6 reshape.103
  349.9 2.9 gather_fusion.3
  352.9 1.7 select_convert_fusion
  354.6 2.5 copy.76
  357.0 8.8 %copy.77 = f32[512,32,48]{2,1,0:T(8,128)} copy(f32[512,32,48]{0,2,1:T(8,128)} %bitcast.76) | data formatting | bytes 6291456 | tf_op jit(solution)/shard_map/convert_element_type | solution.py:66
  365.8 6.5 %fusion.2 = bf16[32,48,512]{1,0,2:T(8,128)(2,1)} fusion(f32[512,32,48]{2,1,0:T(8,128)} %copy.77, f32[48,512]{0,1:T(8,128)S(1)} %broadcast_multiply_fusion), kind=kLoop, calls=%fused_computation.10 | loop fusion | flops 1572864 | bytes 4816896 | tf_op jit(solution)/shard_map/convert_element_type | solution.py:66
  372.3 5.4 %copy.78 = bf16[32,48,512]{2,1,0:T(8,128)(2,1)} copy(bf16[32,48,512]{1,0,2:T(8,128)(2,1)} %fusion.2) | data formatting | bytes 3145728
  377.7 2.9 gather_fusion.1
  380.6 0.2 select_bitcast_fusion
  380.8 1.6 fusion.5
  (21 shorter events, 0.1 us)
Async XLA Ops:
  7.2 16.2 %copy-start = (f32[32,128]{1,0:T(8,128)S(1)}, f32[32,128]{1,0:T(8,128)}, u32[]{:S(2)}) copy-start(f32[32,128]{1,0:T(8,128)} %param.9) | copy-start | bytes 49156
  7.2 103.9 %all-reduce.2.cloned.1.call-start = ((), (), s32[]{:S(2)}) async-start(), calls=%async_computation.5 | async-start | bytes 524288 | tf_op jit(solution)/shard_map/psum | solution.py:32
  14.5 4.8 %copy-start.4 = (s32[512]{0:T(512)S(1)}, s32[512]{0:T(512)}, u32[]{:S(2)}) copy-start(s32[512]{0:T(512)} %param.11) | copy-start | bytes 6148
  130.6 21.1 %all-to-all-start.1 = ((bf16[32,8,2,1536]{3,2,0,1:T(2,128)(2,1)}), bf16[32,8,2,1536]{3,2,0,1:T(2,128)(2,1)S(1)}, u32[]{:S(2)}, u32[]{:S(2)}) async-start(bf16[32,8,2,1536]{3,2,0,1:T(2,128)(2,1)} %copy.65), calls=%async_computation.1 | async-start | bytes 3145728 | tf_op jit(solution)/shard_map/all_to_all | solution.py:46
  151.6 14.2 %all-to-all-start = ((s32[32,1,2]{2,1,0:T(1,128)}), s32[32,1,2]{2,1,0:T(1,128)S(1)}, u32[]{:S(2)}, u32[]{:S(2)}) async-start(s32[32,1,2]{2,1,0:T(1,128)} %constant_dynamic-slice_fusion), calls=%async_computation | async-start | bytes 32768 | tf_op jit(solution)/shard_map/all_to_all | solution.py:29
  165.8 43.8 %all-to-all-start.2 = ((bf16[32,1,2,12288]{3,2,1,0:T(2,128)(2,1)}), bf16[32,1,2,12288]{3,2,1,0:T(2,128)(2,1)S(1)}, u32[]{:S(2)}, u32[]{:S(2)}) async-start(bf16[32,1,2,12288]{3,2,1,0:T(2,128)(2,1)} %reshape.160), calls=%async_computation.2 | async-start | bytes 3145728 | tf_op jit(solution)/shard_map/all_to_all | solution.py:45
  171.8 43.0 %copy-start.3 = (bf16[4,256,256]{2,1,0:T(8,128)(2,1)S(1)}, bf16[4,256,256]{2,1,0:T(8,128)(2,1)}, u32[]{:S(2)}) copy-start(bf16[4,256,256]{2,1,0:T(8,128)(2,1)} %param.10) | copy-start | bytes 1572868
  214.8 3.6 copy-start.2
  300.6 4.8 %copy-start.6 = (s32[128]{0:T(128)S(1)}, s32[128]{0:T(128)}, u32[]{:S(2)}) copy-start(s32[128]{0:T(128)} %param.13) | copy-start | bytes 1540
  300.6 28.8 %all-to-all-start.4 = ((bf16[8,2,49152]{2,1,0:T(2,128)(2,1)}), bf16[8,2,49152]{2,1,0:T(2,128)(2,1)S(1)}, u32[]{:S(2)}, u32[]{:S(2)}) async-start(bf16[8,2,49152]{2,1,0:T(2,128)(2,1)} %reshape.168), calls=%async_computation.4 | async-start | bytes 3145728 | tf_op jit(solution)/shard_map/all_to_all | solution.py:63
  372.3 8.5 %copy-start.5 = (f32[48]{0:T(128)S(1)}, f32[48]{0:T(128)}, u32[]{:S(2)}) copy-start(f32[48]{0:T(128)} %param.12) | copy-start | bytes 580
  372.3 10.1 %copy-start.1 = (f32[32,128]{1,0:T(8,128)S(1)}, f32[32,128]{1,0:T(8,128)}, u32[]{:S(2)}) copy-start(f32[32,128]{1,0:T(8,128)} %param.9) | copy-start | bytes 49156
Sparse Core Ops, SparseCore 0:
  19.4 91.6 all-reduce.1
where the time goes:
time: 391 us; the launch traced here: 389 us
  waiting for transfers between devices  165 us (42%)
  local copies, waits for them, and re-layouts  110 us (28%)
  blocking collectives  44.2 us (11%)
  other arithmetic  23.1 us (6%)
  starting transfers between devices  22.4 us (6%)
  between operations  14.4 us (4%)
  matrix products  10.2 us (3%)
    psum x1, waiting for transfers between devices, local(): summed = lax.psum(jnp.sum(ensemble, axis=0, dtype=jnp.float32), 'member')  83.8 us
    all_to_all x1, blocking collectives, local(): lax.all_to_all(result_rows, 'space', split_axis=0, concat_axis=0, tiled=T...  44.2 us
    all_to_all x1, waiting for transfers between devices, local(): lax.all_to_all(lax.all_to_all(payload, 'member', split_axis=1, concat_axi...  37.2 us
    unnamed x18, local copies, waits for them, and re-layouts  27.6 us
    all_to_all x1, waiting for transfers between devices, local(): lax.all_to_all(halfway, 'member', split_axis=3, concat_axis=1, tiled=True)  24 us
    all_to_all x1, waiting for transfers between devices, local(): lax.all_to_all(payload, 'member', split_axis=1, concat_axis=3, tiled=True)  16.7 us
    all_to_all x1, local copies, waits for them, and re-layouts, local(): lax.all_to_all(halfway, 'member', split_axis=3, concat_axis=1, tiled=True)  14.4 us
    convert_element_type x2, local copies, waits for them, and re-layouts, local(): analysis = (mean[None] + restored.astype(jnp.float32)).astype(jnp.bfloat16)  11.2 us
  transfers between devices with their start and end apart: 5, of which 5 were waited for; matrix products, arithmetic and copies ran while one was open for 3% of the time, Pallas kernels for 0%

commit v1 on v0

--- a/solution.py
+++ b/solution.py
@@ -60,7 +60,16 @@
     result_rows = increment
     result_rows = result_rows.reshape(n_space, 1, slot_cols, members * tracers)
     halfway = lax.all_to_all(result_rows, "space", split_axis=0, concat_axis=0, tiled=True)
-    returned = lax.all_to_all(halfway, "member", split_axis=3, concat_axis=1, tiled=True)
+
+    def set_zones(inner_x):
+        h_now = lax.axis_size("member")
+        p_next = jnp.split(inner_x, h_now, 3)
+        lower = jnp.stack(p_next, axis=0)
+        local_now = lax.all_to_all(lower, "member", split_axis=0, concat_axis=0)
+        block_next = jnp.concatenate(local_now, 1)
+        return block_next
+
+    returned = set_zones(halfway)
     restored = jnp.take(returned.reshape(columns, local_members * tracers), position, axis=0)
     restored = jnp.transpose(restored.reshape(columns, local_members, tracers), (1, 2, 0))
     analysis = (mean[None] + restored.astype(jnp.float32)).astype(jnp.bfloat16)

time: 391 us -> 358 us (0.916)
  local copies, waits for them, and re-layouts: 110 us -> 78.1 us
    all_to_all x2 -> x0, local copies, waits for them, and re-layouts: 25.5 us -> none  [the longest x1 14.4 us: local(): lax.all_to_all(halfway, 'member', split_axis=3, concat_axis=1, tiled=True)]
    unnamed x18 -> x23, local copies, waits for them, and re-layouts: 27.6 us -> 18.3 us
  transfers between devices with their start and end apart: 5 -> 5, of which waited for: 5 -> 5; matrix products, arithmetic and copies ran while one was open for 3% -> 4% of each run, Pallas kernels for 0% -> 0%
where the time goes in v1:
time: 358 us; the launch traced here: 357 us
  waiting for transfers between devices  165 us (46%)
  local copies, waits for them, and re-layouts  78.1 us (22%)
  blocking collectives  44.2 us (12%)
  other arithmetic  23.1 us (6%)
  starting transfers between devices  22.4 us (6%)
  between operations  14.4 us (4%)
  matrix products  10.2 us (3%)
    psum x1, waiting for transfers between devices, local(): summed = lax.psum(jnp.sum(ensemble, axis=0, dtype=jnp.float32), 'member')  83.8 us
    all_to_all x1, blocking collectives, local(): lax.all_to_all(result_rows, 'space', split_axis=0, concat_axis=0, tiled=T...  44.2 us
    all_to_all x1, waiting for transfers between devices, local(): lax.all_to_all(lax.all_to_all(payload, 'member', split_axis=1, concat_axi...  37.2 us
    all_to_all x1, waiting for transfers between devices, set_zones(): local_now = lax.all_to_all(lower, 'member', split_axis=0, concat_axis=0)  24 us
    unnamed x23, local copies, waits for them, and re-layouts  18.3 us
    all_to_all x1, waiting for transfers between devices, local(): lax.all_to_all(payload, 'member', split_axis=1, concat_axis=3, tiled=True)  16.7 us
    convert_element_type x2, local copies, waits for them, and re-layouts, local(): analysis = (mean[None] + restored.astype(jnp.float32)).astype(jnp.bfloat16)  11.2 us
    reshape x1, local copies, waits for them, and re-layouts, local(): result_rows = result_rows.reshape(n_space, 1, slot_cols, members * tracers)  9.29 us
  transfers between devices with their start and end apart: 5, of which 5 were waited for; matrix products, arithmetic and copies ran while one was open for 4% of the time, Pallas kernels for 0%

profile of v1, /device:TPU:64, one launch (start us, length us, event | category | flops | bytes accessed | tf_op | source)
XLA Modules:
  0.0 357.0 jit_solution(11227313663717926934)
XLA Ops:
  7.2 0.0 all-reduce.2.cloned.1.call-start
  7.2 7.2 %copy.54 = bf16[32,48,512]{1,0,2:T(8,128)(2,1)} copy(bf16[32,48,512]{2,1,0:T(8,128)(2,1)} %param.8) | data formatting | bytes 3145728 | tf_op args[0]
  14.5 4.8 %convert_reduce_fusion = f32[48,512]{0,1:T(8,128)} fusion(bf16[32,48,512]{1,0,2:T(8,128)(2,1)} %copy.54), kind=kLoop, calls=%fused_computation.6 | loop fusion | flops 1548288 | bytes 1671168 | tf_op jit(solution)/shard_map/reduce_sum | solution.py:32
  19.2 0.0 all-reduce.2.cloned.1.call-update
  19.3 1.2 reduce-window.6
  20.5 0.2 slice_reduce_fusion
  20.7 0.1 fusion.29
  20.9 2.4 scatter_custom_fusion
  23.3 0.2 convolution_bitcast_fusion
  23.6 3.5 gather_fusion
  27.1 0.1 copy.56
  27.2 83.8 %all-reduce.2.cloned.1.call-done = f32[48,512]{0,1:T(8,128)} async-done(((f32[48,512]{0,1:T(8,128)}), f32[48,512]{0,1:T(8,128)}) %all-reduce.2.cloned.1.call-update) | async-done | bytes 98320 | tf_op jit(solution)/shard_map/psum | solution.py:32
  111.0 1.0 broadcast_multiply_fusion
  112.0 5.8 %fusion.3 = bf16[512,32,48]{2,1,0:T(8,128)(2,1)} fusion(bf16[32,48,512]{1,0,2:T(8,128)(2,1)} %copy.54, f32[32,512]{0,1:T(8,128)S(1)} %copy.56, f32[48,512]{0,1:T(8,128)S(1)} %broadcast_multiply_fusion), kind=kLoop, calls=%fused_computation.11 | loop fusion | flops 3145728 | bytes 3309568 | tf_op jit(solution)/shard_map/transpose | solution.py:41
  117.8 4.4 %copy.57 = bf16[512,32,48]{0,2,1:T(8,128)(2,1)S(1)} copy(bf16[512,32,48]{2,1,0:T(8,128)(2,1)} %fusion.3) | data formatting | bytes 3145728 | tf_op jit(solution)/shard_map/transpose | solution.py:41
  122.3 0.7 copy.58
  123.0 2.9 gather_fusion.2
  125.9 1.6 broadcast_select_fusion
  127.6 0.6 reshape.99
  128.2 2.4 copy.59
  130.6 3.6 %all-to-all-start.1 = ((bf16[32,8,2,1536]{3,2,0,1:T(2,128)(2,1)}), bf16[32,8,2,1536]{3,2,0,1:T(2,128)(2,1)S(1)}, u32[]{:S(2)}, u32[]{:S(2)}) async-start(bf16[32,8,2,1536]{3,2,0,1:T(2,128)(2,1)} %copy.59), calls=%async_computation.1 | async-start | bytes 3145728 | tf_op jit(solution)/shard_map/all_to_all | solution.py:46
  134.1 0.1 select_n.68
  134.3 0.6 constant_dynamic-slice_fusion
  134.9 16.7 %all-to-all-done.1 = bf16[32,8,2,1536]{3,2,0,1:T(2,128)(2,1)S(1)} async-done(((bf16[32,8,2,1536]{3,2,0,1:T(2,128)(2,1)}), bf16[32,8,2,1536]{3,2,0,1:T(2,128)(2,1)S(1)}, u32[]{:S(2)}, u32[]{:S(2)}) %all-to-all-start.1) | async-done | bytes 1572896 | tf_op jit(solution)/shard_map/all_to_all | solution.py:46
  151.6 8.0 %all-to-all-start = ((s32[32,1,2]{2,1,0:T(1,128)}), s32[32,1,2]{2,1,0:T(1,128)S(1)}, u32[]{:S(2)}, u32[]{:S(2)}) async-start(s32[32,1,2]{2,1,0:T(1,128)} %constant_dynamic-slice_fusion), calls=%async_computation | async-start | bytes 32768 | tf_op jit(solution)/shard_map/all_to_all | solution.py:29
  159.6 1.3 copy.85
  160.9 2.1 reshape.159
  163.0 2.8 all-to-all-done
  165.8 6.0 %all-to-all-start.2 = ((bf16[32,1,2,12288]{3,2,1,0:T(2,128)(2,1)}), bf16[32,1,2,12288]{3,2,1,0:T(2,128)(2,1)S(1)}, u32[]{:S(2)}, u32[]{:S(2)}) async-start(bf16[32,1,2,12288]{3,2,1,0:T(2,128)(2,1)} %reshape.159), calls=%async_computation.2 | async-start | bytes 3145728 | tf_op jit(solution)/shard_map/all_to_all | solution.py:45
  171.8 0.2 compare_reduce_fusion.3
  172.0 0.1 eq.105
  172.1 0.1 eq.108
  172.2 0.1 eq.111
  172.4 0.1 eq.99
  172.5 37.2 %all-to-all-done.2 = bf16[32,1,2,12288]{3,2,1,0:T(2,128)(2,1)S(1)} async-done(((bf16[32,1,2,12288]{3,2,1,0:T(2,128)(2,1)}), bf16[32,1,2,12288]{3,2,1,0:T(2,128)(2,1)S(1)}, u32[]{:S(2)}, u32[]{:S(2)}) %all-to-all-start.2) | async-done | bytes 1572896 | tf_op jit(solution)/shard_map/all_to_all | solution.py:45
  209.6 5.2 %reshape.100 = bf16[64,256,48]{2,1,0:T(8,128)(2,1)} reshape(bf16[32,1,2,12288]{3,2,1,0:T(2,128)(2,1)S(1)} %all-to-all-done.2) | data formatting | bytes 3145728 | tf_op jit(solution)/shard_map/reshape | solution.py:52
  214.8 3.6 %fusion.16 = f32[64,48,256]{2,1,0:T(8,128)S(1)} fusion(bf16[64,256,48]{2,1,0:T(8,128)(2,1)} %reshape.100, bf16[4,256,256]{2,1,0:T(8,128)(2,1)S(1)} %copy-done.3), kind=kOutput, calls=%fused_computation.38 | convolution fusion | flops 402653184 | bytes 4849664 | tf_op jit(solution)/shard_map/jk,cjt->ckt/dot_general | solution.py:55
  218.4 1.3 fusion.18
  219.7 1.3 fusion.20
  221.0 2.3 fusion.4
  223.3 3.2 copy.66
  226.4 9.3 %reshape.101 = bf16[32,1,2,12288]{3,2,0,1:T(2,128)(2,1)S(1)} reshape(bf16[64,256,48]{2,1,0:T(8,128)(2,1)} %copy.66) | data formatting | bytes 3145728 | tf_op jit(solution)/shard_map/reshape | solution.py:61
  235.7 44.2 %all_to_all.39 = bf16[32,1,2,12288]{3,2,1,0:T(2,128)(2,1)S(1)} all-to-all(bf16[32,1,2,12288]{3,2,1,0:T(2,128)(2,1)S(1)} %bitcast.121), channel_id=1, replica_groups=mesh['member'=8,'space'=32] {'space'}, dimensions={0} | all-to-all | bytes 3145728 | tf_op jit(solution)/shard_map/all_to_all | solution.py:62
  280.0 0.8 fusion.14
  280.8 0.8 fusion.13
  281.6 0.8 fusion.12
  282.4 0.8 fusion.11
  283.2 0.8 fusion.10
  284.1 0.8 fusion.9
  284.9 0.8 fusion.8
  285.7 0.8 fusion.7
  286.5 4.8 %all-to-all-start.4 = ((bf16[8,32,1,2,1536]{4,3,1,2,0:T(2,128)(2,1)}), bf16[8,32,1,2,1536]{4,3,1,2,0:T(2,128)(2,1)S(1)}, u32[]{:S(2)}, u32[]{:S(2)}) async-start(bf16[8,32,1,2,1536]{4,3,1,2,0:T(2,128)(2,1)} %fusion.7), calls=%async_computation.4 | async-start | bytes 3145728 | tf_op jit(solution)/shard_map/all_to_all | solution.py:68
  291.4 24.0 %all-to-all-done.4 = bf16[8,32,1,2,1536]{4,3,1,2,0:T(2,128)(2,1)S(1)} async-done(((bf16[8,32,1,2,1536]{4,3,1,2,0:T(2,128)(2,1)}), bf16[8,32,1,2,1536]{4,3,1,2,0:T(2,128)(2,1)S(1)}, u32[]{:S(2)}, u32[]{:S(2)}) %all-to-all-start.4) | async-done | bytes 1572896 | tf_op jit(solution)/shard_map/all_to_all | solution.py:68
  315.3 1.6 copy.75
  317.0 0.6 reshape_reshape.3
  317.6 2.9 gather_fusion.3
  320.6 1.7 select_convert_fusion
  322.3 2.5 copy.76
  324.7 8.8 %copy.77 = f32[512,32,48]{2,1,0:T(8,128)} copy(f32[512,32,48]{0,2,1:T(8,128)} %bitcast.110) | data formatting | bytes 6291456 | tf_op jit(solution)/shard_map/convert_element_type | solution.py:75
  333.5 6.5 %fusion.2 = bf16[32,48,512]{1,0,2:T(8,128)(2,1)} fusion(f32[512,32,48]{2,1,0:T(8,128)} %copy.77, f32[48,512]{0,1:T(8,128)S(1)} %broadcast_multiply_fusion), kind=kLoop, calls=%fused_computation.10 | loop fusion | flops 1572864 | bytes 4816896 | tf_op jit(solution)/shard_map/convert_element_type | solution.py:75
  340.0 5.3 %copy.78 = bf16[32,48,512]{2,1,0:T(8,128)(2,1)} copy(bf16[32,48,512]{1,0,2:T(8,128)(2,1)} %fusion.2) | data formatting | bytes 3145728
  345.3 3.0 gather_fusion.1
  348.3 0.2 select_bitcast_fusion
  348.5 1.6 fusion.5
  (25 shorter events, 0.1 us)
Async XLA Ops:
  7.2 16.2 %copy-start = (f32[32,128]{1,0:T(8,128)S(1)}, f32[32,128]{1,0:T(8,128)}, u32[]{:S(2)}) copy-start(f32[32,128]{1,0:T(8,128)} %param.9) | copy-start | bytes 49156
  7.2 103.9 %all-reduce.2.cloned.1.call-start = ((), (), s32[]{:S(2)}) async-start(), calls=%async_computation.5 | async-start | bytes 524288 | tf_op jit(solution)/shard_map/psum | solution.py:32
  14.5 4.8 %copy-start.4 = (s32[512]{0:T(512)S(1)}, s32[512]{0:T(512)}, u32[]{:S(2)}) copy-start(s32[512]{0:T(512)} %param.11) | copy-start | bytes 6148
  130.6 21.1 %all-to-all-start.1 = ((bf16[32,8,2,1536]{3,2,0,1:T(2,128)(2,1)}), bf16[32,8,2,1536]{3,2,0,1:T(2,128)(2,1)S(1)}, u32[]{:S(2)}, u32[]{:S(2)}) async-start(bf16[32,8,2,1536]{3,2,0,1:T(2,128)(2,1)} %copy.59), calls=%async_computation.1 | async-start | bytes 3145728 | tf_op jit(solution)/shard_map/all_to_all | solution.py:46
  151.6 14.2 %all-to-all-start = ((s32[32,1,2]{2,1,0:T(1,128)}), s32[32,1,2]{2,1,0:T(1,128)S(1)}, u32[]{:S(2)}, u32[]{:S(2)}) async-start(s32[32,1,2]{2,1,0:T(1,128)} %constant_dynamic-slice_fusion), calls=%async_computation | async-start | bytes 32768 | tf_op jit(solution)/shard_map/all_to_all | solution.py:29
  165.8 43.8 %all-to-all-start.2 = ((bf16[32,1,2,12288]{3,2,1,0:T(2,128)(2,1)}), bf16[32,1,2,12288]{3,2,1,0:T(2,128)(2,1)S(1)}, u32[]{:S(2)}, u32[]{:S(2)}) async-start(bf16[32,1,2,12288]{3,2,1,0:T(2,128)(2,1)} %reshape.159), calls=%async_computation.2 | async-start | bytes 3145728 | tf_op jit(solution)/shard_map/all_to_all | solution.py:45
  172.5 42.3 %copy-start.3 = (bf16[4,256,256]{2,1,0:T(8,128)(2,1)S(1)}, bf16[4,256,256]{2,1,0:T(8,128)(2,1)}, u32[]{:S(2)}) copy-start(bf16[4,256,256]{2,1,0:T(8,128)(2,1)} %param.10) | copy-start | bytes 1572868
  214.8 3.6 %copy-start.2 = (bf16[64,256,48]{2,1,0:T(8,128)(2,1)S(1)}, bf16[64,256,48]{2,1,0:T(8,128)(2,1)}, u32[]{:S(2)}) copy-start(bf16[64,256,48]{2,1,0:T(8,128)(2,1)} %reshape.100) | copy-start | bytes 4718596
  286.5 4.8 %copy-start.6 = (s32[128]{0:T(128)S(1)}, s32[128]{0:T(128)}, u32[]{:S(2)}) copy-start(s32[128]{0:T(128)} %param.13) | copy-start | bytes 1540
  286.5 28.8 %all-to-all-start.4 = ((bf16[8,32,1,2,1536]{4,3,1,2,0:T(2,128)(2,1)}), bf16[8,32,1,2,1536]{4,3,1,2,0:T(2,128)(2,1)S(1)}, u32[]{:S(2)}, u32[]{:S(2)}) async-start(bf16[8,32,1,2,1536]{4,3,1,2,0:T(2,128)(2,1)} %fusion.7), calls=%async_computation.4 | async-start | bytes 3145728 | tf_op jit(solution)/shard_map/all_to_all | solution.py:68
  345.3 3.2 copy-start.5
  348.3 1.8 copy-start.1
Sparse Core Ops, SparseCore 0:
  19.4 91.6 all-reduce.1
